TPU v7x, 512 devices: a whole 4x4x16 slice. The times are simulated.
512 devices in a mesh: gx: 8 (over x, core), gy: 4 (over y), gz: 16 (over z).
Axes of the slice: x: 4, y: 4, z: 16, core: 2. Of those that a mesh axis runs over, the one named last changes fastest.
Arguments:
- multipoles: bfloat16 [289, 262144], P(None, ('gx', 'gy', 'gz')), may hold values from -6 to 6
- up_shift: bfloat16 [8, 289, 289], replicated, may hold values from -0.125 to 0.125
- down_shift: bfloat16 [8, 289, 289], replicated, may hold values from -0.375 to 0.375
- far_shift: bfloat16 [8, 289, 289], replicated, may hold values from -0.09375 to 0.09375
- send_list: int32 [8, 64, 64, 16], P('gx', ('gy', 'gz')), may hold values from 0 to 511
- leaf_src: int32 [16, 262144], P(None, ('gx', 'gy', 'gz')), may hold values from 0 to 1535
- leaf_kind: int32 [16, 262144], P(None, ('gx', 'gy', 'gz')), may hold values from 0 to 7
- coarse_src: int32 [8, 64], replicated, may hold values from 0 to 63
- coarse_kind: int32 [8, 64], replicated, may hold values from 0 to 7
Outputs:
- leaf_local: bfloat16 [289, 262144], P(None, ('gx', 'gy', 'gz'))
All inputs are finite; a program needn't handle non-finite values.
Results may differ from a plain program's by a relative error of at most 0.014.
Values may be sent and summed in bfloat16 or wider, within the bound.
No kernel may reach another device: no remote copies, remote signals or barrier semaphores. Data moves between devices by JAX's collectives and lax.ppermute only.
A program may use at most 128 MiB of HBM per device.

v0:
```python
import jax
import jax.numpy as jnp
from jax import lax
from jax.sharding import PartitionSpec as P

LOCAL_LEVELS = 3


def lift_level(children, up_shift):
    coefs = children.shape[0]
    count = children.shape[1] // 8
    child_stack = children.reshape(coefs, count, 8).transpose(2, 0, 1).reshape(8 * coefs, count)
    shift_table = up_shift.transpose(1, 0, 2).reshape(coefs, 8 * coefs)
    return jnp.dot(shift_table, child_stack, preferred_element_type=jnp.float32)


def lower_level(parent, down_shift):
    coefs = parent.shape[0]
    count = parent.shape[1]
    spread = jnp.dot(
        down_shift.reshape(8 * coefs, coefs), parent, preferred_element_type=jnp.float32
    )
    return spread.reshape(8, coefs, count).transpose(1, 2, 0).reshape(coefs, 8 * count)


def gather_columns(column_block, axes):
    group = lax.axis_size(axes)
    width = column_block.shape[1]
    spread = jnp.broadcast_to(column_block[:, None, :], (column_block.shape[0], group, width))
    spread = spread.reshape(column_block.shape[0], group * width)
    return lax.all_to_all(spread, axes, split_axis=1, concat_axis=1, tiled=True)


def on_device(
    multipoles,
    up_shift,
    down_shift,
    far_shift,
    send_list,
    leaf_src,
    leaf_kind,
    coarse_src,
    coarse_kind,
):
    coefs = multipoles.shape[0]
    kind_count = far_shift.shape[0]
    flat_index = lax.axis_index(("gx", "gy", "gz"))
    coarse_box = flat_index // 8
    octant = flat_index % 8
    peer_count = lax.axis_size(("gy", "gz"))
    slot_count = send_list.shape[3]
    send_order = send_list.reshape(peer_count * slot_count)
    outgoing = jnp.take(multipoles, send_order, axis=1)
    arrived = lax.all_to_all(outgoing, ("gy", "gz"), split_axis=1, concat_axis=1, tiled=True)
    upward = multipoles
    for level in range(LOCAL_LEVELS):
        upward = lift_level(upward, up_shift).astype(jnp.bfloat16)
    row_boxes = gather_columns(upward, "gz")
    row_multi = lift_level(row_boxes, up_shift).astype(jnp.bfloat16)
    coarse_multi = gather_columns(row_multi, ("gx", "gy"))
    coarse_cols = coarse_src[:, coarse_box]
    coarse_kinds = coarse_kind[:, coarse_box]
    list_len = coarse_cols.shape[0]
    coarse_picked = jnp.take(coarse_multi, coarse_cols, axis=1)
    stacked = (
        jnp.take(far_shift, coarse_kinds, axis=0)
        .transpose(1, 0, 2)
        .reshape(coefs, list_len * coefs)
    )
    column_vec = coarse_picked.transpose(1, 0).reshape(list_len * coefs, 1)
    coarse_local = jnp.dot(stacked, column_vec, preferred_element_type=jnp.float32).astype(
        jnp.bfloat16
    )
    downward = jnp.dot(down_shift[octant], coarse_local, preferred_element_type=jnp.float32).astype(
        jnp.bfloat16
    )
    for level in range(LOCAL_LEVELS - 1):
        downward = lower_level(downward, down_shift).astype(jnp.bfloat16)
    chain_part = lower_level(downward, down_shift)
    buffer = jnp.concatenate([multipoles, arrived], axis=1)
    leaf_count = leaf_src.shape[1]
    picked = jnp.take(buffer, leaf_src, axis=1)
    kind_range = jnp.arange(kind_count, dtype=jnp.int32)
    kind_hot = (leaf_kind[None, :, :] == kind_range[:, None, None]).astype(jnp.bfloat16)
    grouped = jnp.einsum("plt,klt->kpt", picked, kind_hot, preferred_element_type=jnp.float32)
    grouped = grouped.reshape(kind_count * coefs, leaf_count)
    upper_part = grouped.astype(jnp.bfloat16)
    lower_part = (grouped - upper_part.astype(jnp.float32)).astype(jnp.bfloat16)
    shift_table = far_shift.transpose(1, 0, 2).reshape(coefs, kind_count * coefs)
    far_total = jnp.dot(shift_table, upper_part, preferred_element_type=jnp.float32)
    far_total = far_total + jnp.dot(shift_table, lower_part, preferred_element_type=jnp.float32)
    return (chain_part + far_total).astype(jnp.bfloat16)


def solution(mesh):
    in_specs = (
        P(None, ("gx", "gy", "gz")),
        P(),
        P(),
        P(),
        P("gx", ("gy", "gz"), None, None),
        P(None, ("gx", "gy", "gz")),
        P(None, ("gx", "gy", "gz")),
        P(),
        P(),
    )
    out_specs = P(None, ("gx", "gy", "gz"))
    return jax.shard_map(
        on_device, mesh=mesh, in_specs=in_specs, out_specs=out_specs, check_vma=False
    )
```

profile of v0, /device:TPU:8, one launch (start us, length us, event | category | flops | bytes accessed | tf_op | source)
XLA Modules:
  0.0 159.2 jit_solution(3946871346502079837)
XLA Ops:
  1.2 4.2 %reshape.156 = bf16[289,2312]{1,0:T(8,128)(2,1)} reshape(bf16[289,8,289]{2,1,0:T(8,128)(2,1)} %bitcast.158) | data formatting | bytes 2672672 | tf_op jit(solution)/shard_map/reshape | solution.py:13
  6.9 1.9 %convolution_reduce_fusion.1 = bf16[289]{0:T(512)(128)(2,1)S(1)} fusion(bf16[2312,1]{0,1:T(2,128)(2,1)S(1)} %reshape.200, bf16[289,2312]{1,0:T(8,128)(2,1)} %reshape.156), kind=kOutput, calls=%fused_computation.45 | convolution fusion | flops 1336336 | bytes 1341538 | tf_op jit(solution)/shard_map/dot_general | solution.py:14
  9.4 15.2 %all-to-all-start = ((bf16[289,16,1]{0,2,1:T(2,128)(2,1)}), bf16[289,16,1]{0,2,1:T(2,128)(2,1)S(1)}, u32[]{:S(2)}, u32[]{:S(2)}) async-start(bf16[289,16,1]{0,2,1:T(2,128)(2,1)} %reshape.157), calls=%async_computation | async-start | bytes 49152 | tf_op jit(solution)/shard_map/all_to_all | solution.py:31
  24.8 3.9 %gather_fusion.2 = bf16[1024,289]{1,0:T(8,128)(2,1)S(1)} fusion(bf16[289,512]{0,1:T(8,128)(2,1)S(1)} %copy.69, s32[1024]{0:T(1024)S(1)} %broadcast_clamp_fusion.1), kind=kCustom, calls=%fused_computation.2 | custom fusion | bytes 1187840 | tf_op jit(solution)/shard_map/jit(_take)/gather | solution.py:53
  29.9 7.2 %all-to-all-done = bf16[289,16,1]{0,2,1:T(2,128)(2,1)S(1)} async-done(((bf16[289,16,1]{0,2,1:T(2,128)(2,1)}), bf16[289,16,1]{0,2,1:T(2,128)(2,1)S(1)}, u32[]{:S(2)}, u32[]{:S(2)}) %all-to-all-start) | async-done | bytes 9280 | tf_op jit(solution)/shard_map/all_to_all | solution.py:31
  37.1 2.2 %fusion.60 = bf16[289,2]{0,1:T(2,128)(2,1)S(1)} fusion(bf16[289,8,289]{2,1,0:T(8,128)(2,1)} %bitcast.159, bf16[289,2,8]{0,2,1:T(8,128)(2,1)S(1)} %bitcast.168), kind=kOutput, calls=%fused_computation.46 | convolution fusion | flops 2673250 | bytes 1346740 | tf_op jit(solution)/shard_map/dot_general | solution.py:14
  40.0 7.5 %all-to-all-start.1 = ((bf16[289,32,2]{0,2,1:T(2,128)(2,1)}), bf16[289,32,2]{0,2,1:T(2,128)(2,1)S(1)}, u32[]{:S(2)}, u32[]{:S(2)}) async-start(bf16[289,32,2]{0,2,1:T(2,128)(2,1)} %broadcast_in_dim.57), calls=%async_computation.1 | async-start | bytes 98304 | tf_op jit(solution)/shard_map/all_to_all | solution.py:31
  47.6 6.2 %all-to-all-done.1 = bf16[289,32,2]{0,2,1:T(2,128)(2,1)S(1)} async-done(((bf16[289,32,2]{0,2,1:T(2,128)(2,1)}), bf16[289,32,2]{0,2,1:T(2,128)(2,1)S(1)}, u32[]{:S(2)}, u32[]{:S(2)}) %all-to-all-start.1) | async-done | bytes 37024 | tf_op jit(solution)/shard_map/all_to_all | solution.py:31
  53.7 7.5 %all-to-all-start.2 = ((bf16[289,64,16]{0,2,1:T(8,128)(2,1)}), bf16[289,64,16]{0,2,1:T(8,128)(2,1)S(1)}, u32[]{:S(2)}, u32[]{:S(2)}) async-start(bf16[289,64,16]{0,2,1:T(8,128)(2,1)} %broadcast_select_fusion), calls=%async_computation.2 | async-start | bytes 1572864 | tf_op jit(solution)/shard_map/all_to_all | solution.py:54
  61.2 3.1 %copy.76 = bf16[8,289,289]{1,0,2:T(8,128)(2,1)} copy(bf16[8,289,289]{2,0,1:T(8,128)(2,1)S(1)} %copy-done.3) | data formatting | bytes 2672672 | tf_op args[2]
  64.4 4.2 %reshape.159 = bf16[2312,289]{0,1:T(8,128)(2,1)} reshape(bf16[8,289,289]{1,0,2:T(8,128)(2,1)} %copy.76) | data formatting | bytes 2672672 | tf_op jit(solution)/shard_map/reshape | solution.py:21
  69.9 6.8 %gather_fusion = bf16[8,289,289]{2,0,1:T(8,128)(2,1)} fusion(bf16[8,289,289]{2,0,1:T(8,128)(2,1)S(1)} %copy-done, s32[1024]{0:T(1024)S(1)} %pad_clamp_fusion.1), kind=kCustom, calls=%fused_computation | custom fusion | bytes 2672704 | tf_op jit(solution)/shard_map/jit(_take)/gather | solution.py:66
  76.7 3.2 %copy.95 = bf16[289,8,289]{0,1,2:T(8,128)(2,1)} copy(bf16[289,8,289]{2,1,0:T(8,128)(2,1)S(1)} %bitcast.156) | data formatting | bytes 2672672 | tf_op jit(solution)/shard_map/transpose | solution.py:89
  80.3 1.9 %constant_dynamic-slice_fusion = bf16[1,289,289]{2,0,1:T(2,128)(2,1)S(1)} fusion(bf16[8,289,289]{2,0,1:T(8,128)(2,1)} %param.11, s32[]{:T(128)S(6)} %select_n.79), kind=kLoop, calls=%fused_computation.77 | loop fusion | bytes 334088 | tf_op jit(solution)/shard_map/dynamic_slice | solution.py:74
  82.2 3.0 %select_bitcast_fusion = bf16[289,8,289]{2,1,0:T(8,128)(2,1)} fusion(bf16[8,289,289]{2,0,1:T(8,128)(2,1)} %gather_fusion, pred[8]{0:T(512)(128)(4,1)S(1)} %get-tuple-element.6), kind=kLoop, calls=%fused_computation.21 | loop fusion | flops 668168 | bytes 2672680 | tf_op jit(solution)/shard_map/jit(_take)/select_n | solution.py:66
  85.9 2.2 %fusion.57 = bf16[289]{0:T(512)(128)(2,1)S(1)} fusion(bf16[289,8,289]{2,1,0:T(8,128)(2,1)} %select_bitcast_fusion, bf16[8,289,1]{1,0,2:T(8,128)(2,1)S(1)} %select_bitcast_fusion.1), kind=kOutput, calls=%fused_computation.43 | convolution fusion | flops 1336336 | bytes 1341538 | tf_op jit(solution)/shard_map/dot_general | solution.py:71
  88.4 2.2 %fusion.8 = bf16[1,8,289]{2,0,1:T(2,128)(2,1)S(1)} fusion(bf16[289,1,1]{0,1,2:T(2,128)(2,1)S(1)} %reshape.207, bf16[8,289,289]{2,0,1:T(8,128)(2,1)} %param.11), kind=kOutput, calls=%fused_computation.17 | convolution fusion | flops 1336336 | bytes 1341538 | tf_op jit(solution)/shard_map/dot_general | solution.py:20
  92.2 1.5 reshape.160
  94.8 8.9 %all-to-all-done.2 = bf16[289,64,16]{0,2,1:T(8,128)(2,1)S(1)} async-done(((bf16[289,64,16]{0,2,1:T(8,128)(2,1)}), bf16[289,64,16]{0,2,1:T(8,128)(2,1)S(1)}, u32[]{:S(2)}, u32[]{:S(2)}) %all-to-all-start.2) | async-done | bytes 591904 | tf_op jit(solution)/shard_map/all_to_all | solution.py:54
  103.9 33.2 %gather_fusion.3 = bf16[8192,289]{1,0:T(8,128)(2,1)} fusion(bf16[289,1536]{0,1:T(8,128)(2,1)S(1)} %pad_maximum_fusion, s32[8192]{0:T(1024)S(1)} %broadcast_clamp_fusion), kind=kCustom, calls=%fused_computation.3 | custom fusion | bytes 9502720 | tf_op jit(solution)/shard_map/jit(_take)/gather | solution.py:82
  137.1 10.0 %fusion = f32[512,8,289]{2,1,0:T(8,128)} fusion(bf16[16,512,289]{2,1,0:T(8,128)(2,1)} %bitcast.162, pred[16,512]{0,1:T(8,128)(4,1)S(1)} %copy.78, s32[16,512]{0,1:T(8,128)S(1)} %copy-done.7), kind=kOutput, calls=%fused_computation.4 | convolution fusion | flops 40312832 | bytes 9510912 | tf_op jit(solution)/shard_map/plt,klt->kpt/dot_general | solution.py:85
  147.1 6.5 %copy.84 = f32[512,8,289]{0,1,2:T(8,128)} copy(f32[512,8,289]{2,1,0:T(8,128)} %fusion) | data formatting | bytes 9469952 | tf_op jit(solution)/shard_map/plt,klt->kpt/dot_general | solution.py:85
  153.6 3.5 %convolution_bitcast_fusion.1 = f32[512,289]{0,1:T(8,128)S(1)} fusion(bf16[289,8,289]{0,1,2:T(8,128)(2,1)S(1)} %copy-done.5, f32[512,8,289]{0,1,2:T(8,128)} %copy.84), kind=kOutput, calls=%fused_computation.29 | convolution fusion | flops 684204032 | bytes 6663184 | tf_op jit(solution)/shard_map/dot_general | solution.py:90
  157.5 1.7 %fusion.30 = bf16[289,512]{1,0:T(8,128)(2,1)} fusion(f32[289,512]{1,0:T(8,128)S(1)} %copy-done.6, f32[512,289]{0,1:T(8,128)S(1)} %convolution_bitcast_fusion.1, bf16[289,8,289]{0,1,2:T(8,128)(2,1)S(1)} %copy-done.5, f32[512,8,289]{0,1,2:T(8,128)S(1)} %copy-done.1), kind=kOutput, calls=%fused_computation.33 | convolution fusion | flops 689382912 | bytes 7550992 | tf_op jit(solution)/shard_map/dot_general | solution.py:91
  (62 shorter events, 11.2 us)
Async XLA Ops:
  1.2 4.2 %copy-start.4 = (bf16[8,289,289]{2,0,1:T(8,128)(2,1)S(1)}, bf16[8,289,289]{2,0,1:T(8,128)(2,1)}, u32[]{:S(2)}) copy-start(bf16[8,289,289]{2,0,1:T(8,128)(2,1)} %param.10) | copy-start | bytes 4009012
  6.1 18.4 %copy-start.10 = (s32[1,1,64,16]{2,3,1,0:T(8,128)S(1)}, s32[1,1,64,16]{2,3,1,0:T(8,128)}, u32[]{:S(2)}) copy-start(s32[1,1,64,16]{2,3,1,0:T(8,128)} %param.13) | copy-start | bytes 12292
  9.4 27.8 %all-to-all-start = ((bf16[289,16,1]{0,2,1:T(2,128)(2,1)}), bf16[289,16,1]{0,2,1:T(2,128)(2,1)S(1)}, u32[]{:S(2)}, u32[]{:S(2)}) async-start(bf16[289,16,1]{0,2,1:T(2,128)(2,1)} %reshape.157), calls=%async_computation | async-start | bytes 49152 | tf_op jit(solution)/shard_map/all_to_all | solution.py:31
  28.8 18.7 %copy-start.8 = (s32[16,512]{1,0:T(8,128)S(1)}, s32[16,512]{1,0:T(8,128)}, u32[]{:S(2)}) copy-start(s32[16,512]{1,0:T(8,128)} %param.14) | copy-start | bytes 98308
  37.1 24.1 %copy-start.3 = (bf16[8,289,289]{2,0,1:T(8,128)(2,1)S(1)}, bf16[8,289,289]{2,0,1:T(8,128)(2,1)}, u32[]{:S(2)}) copy-start(bf16[8,289,289]{2,0,1:T(8,128)(2,1)} %param.11) | copy-start | bytes 4009012
  40.0 13.7 %all-to-all-start.1 = ((bf16[289,32,2]{0,2,1:T(2,128)(2,1)}), bf16[289,32,2]{0,2,1:T(2,128)(2,1)S(1)}, u32[]{:S(2)}, u32[]{:S(2)}) async-start(bf16[289,32,2]{0,2,1:T(2,128)(2,1)} %broadcast_in_dim.57), calls=%async_computation.1 | async-start | bytes 98304 | tf_op jit(solution)/shard_map/all_to_all | solution.py:31
  53.7 50.0 %all-to-all-start.2 = ((bf16[289,64,16]{0,2,1:T(8,128)(2,1)}), bf16[289,64,16]{0,2,1:T(8,128)(2,1)S(1)}, u32[]{:S(2)}, u32[]{:S(2)}) async-start(bf16[289,64,16]{0,2,1:T(8,128)(2,1)} %broadcast_select_fusion), calls=%async_computation.2 | async-start | bytes 1572864 | tf_op jit(solution)/shard_map/all_to_all | solution.py:54
  64.4 4.2 %copy-start.9 = (s32[16,512]{1,0:T(8,128)S(1)}, s32[16,512]{1,0:T(8,128)}, u32[]{:S(2)}) copy-start(s32[16,512]{1,0:T(8,128)} %param.15) | copy-start | bytes 98308
  64.4 5.3 %copy-start.11 = (s32[8,64]{1,0:T(8,128)S(1)}, s32[8,64]{1,0:T(8,128)}, u32[]{:S(2)}) copy-start(s32[8,64]{1,0:T(8,128)} %param.17) | copy-start | bytes 6148
  64.4 5.5 %copy-start = (bf16[8,289,289]{2,0,1:T(8,128)(2,1)S(1)}, bf16[8,289,289]{2,0,1:T(8,128)(2,1)}, u32[]{:S(2)}) copy-start(bf16[8,289,289]{2,0,1:T(8,128)(2,1)} %param.12) | copy-start | bytes 4009012
  76.7 3.2 %copy-start.12 = (s32[8,64]{1,0:T(8,128)S(1)}, s32[8,64]{1,0:T(8,128)}, u32[]{:S(2)}) copy-start(s32[8,64]{1,0:T(8,128)} %param.16) | copy-start | bytes 6148
  85.9 4.6 %copy-start.2 = (bf16[2312,289]{0,1:T(8,128)(2,1)S(1)}, bf16[2312,289]{0,1:T(8,128)(2,1)}, u32[]{:S(2)}) copy-start(bf16[2312,289]{0,1:T(8,128)(2,1)} %reshape.159) | copy-start | bytes 4009012
  103.9 33.2 %copy-start.7 = (s32[16,512]{0,1:T(8,128)S(1)}, s32[16,512]{0,1:T(8,128)}, u32[]{:S(2)}) copy-start(s32[16,512]{0,1:T(8,128)} %copy.77) | copy-start | bytes 98308
  147.0 6.5 %copy-start.5 = (bf16[289,8,289]{0,1,2:T(8,128)(2,1)S(1)}, bf16[289,8,289]{0,1,2:T(8,128)(2,1)}, u32[]{:S(2)}) copy-start(bf16[289,8,289]{0,1,2:T(8,128)(2,1)} %copy.95) | copy-start | bytes 4009012
  153.6 3.8 %copy-start.1 = (f32[512,8,289]{0,1,2:T(8,128)S(1)}, f32[512,8,289]{0,1,2:T(8,128)}, u32[]{:S(2)}) copy-start(f32[512,8,289]{0,1,2:T(8,128)} %copy.84) | copy-start | bytes 14204932
  153.6 3.9 %copy-start.6 = (f32[289,512]{1,0:T(8,128)S(1)}, f32[289,512]{1,0:T(8,128)}, u32[]{:S(2)}) copy-start(f32[289,512]{1,0:T(8,128)} %copy.89) | copy-start | bytes 1775620
where the time goes:
time: 160 us; the launch traced here: 159 us
  local copies, waits for them, and re-layouts  74.7 us (47%)
  starting transfers between devices  30.2 us (19%)
  matrix products  26.7 us (17%)
  waiting for transfers between devices  22.3 us (14%)
  other arithmetic  4.96 us (3%)
    gather x1, local copies, waits for them, and re-layouts, on_device(): picked = jnp.take(buffer, leaf_src, axis=1)  33.2 us
    all_to_all x2, starting transfers between devices, gather_columns(): return lax.all_to_all(spread, axes, split_axis=1, concat_axis=1, tiled=True)  22.7 us
    all_to_all x2, waiting for transfers between devices, gather_columns(): return lax.all_to_all(spread, axes, split_axis=1, concat_axis=1, tiled=True)  13.4 us
    dot_general x1, matrix products, on_device(): jnp.einsum('plt,klt->kpt', picked, kind_hot, preferred_element_type=jnp.f...  9.96 us
    all_to_all x1, waiting for transfers between devices, on_device(): lax.all_to_all(outgoing, ('gy', 'gz'), split_axis=1, concat_axis=1, tiled...  8.93 us
    all_to_all x1, starting transfers between devices, on_device(): lax.all_to_all(outgoing, ('gy', 'gz'), split_axis=1, concat_axis=1, tiled...  7.45 us
    gather x1, local copies, waits for them, and re-layouts, on_device(): jnp.take(far_shift, coarse_kinds, axis=0).transpose(1, 0, 2)  6.81 us
    dot_general x1, local copies, waits for them, and re-layouts, on_device(): jnp.einsum('plt,klt->kpt', picked, kind_hot, preferred_element_type=jnp.f...  6.5 us
  transfers between devices with their start and end apart: 3, of which 3 were waited for; matrix products, arithmetic and copies ran while one was open for 24% of the time, Pallas kernels for 0%

commit v1 on v0

--- a/solution.py
+++ b/solution.py
@@ -28,7 +28,10 @@
     width = column_block.shape[1]
     spread = jnp.broadcast_to(column_block[:, None, :], (column_block.shape[0], group, width))
     spread = spread.reshape(column_block.shape[0], group * width)
-    return lax.all_to_all(spread, axes, split_axis=1, concat_axis=1, tiled=True)
+    return jnp.concatenate(
+        lax.all_to_all(jnp.stack(jnp.split(spread, lax.axis_size(axes), axis=1)), axes, 0, 0),
+        axis=1,
+    )
 
 
 def on_device(

time: 160 us -> 178 us (1.11)
  local copies, waits for them, and re-layouts: 74.7 us -> 93 us
    unnamed x32 -> x60, local copies, waits for them, and re-layouts: 5.69 us -> 24.9 us
    all_to_all x1, waiting for transfers between devices: 8.93 us -> 11.3 us  [on_device(): lax.all_to_all(outgoing, ('gy', 'gz'), split_axis=1, concat_axis=1, tiled...]
  transfers between devices with their start and end apart: 3 -> 3, of which waited for: 3 -> 3; matrix products, arithmetic and copies ran while one was open for 24% -> 21% of each run, Pallas kernels for 0% -> 0%
where the time goes in v1:
time: 178 us
  local copies, waits for them, and re-layouts  93 us (52%)
  starting transfers between devices  30.4 us (17%)
  matrix products  25.2 us (14%)
  waiting for transfers between devices  23.6 us (13%)
  other arithmetic  4.98 us (3%)
    gather x1, local copies, waits for them, and re-layouts, on_device(): picked = jnp.take(buffer, leaf_src, axis=1)  33.2 us
    unnamed x60, local copies, waits for them, and re-layouts  24.9 us
    all_to_all x2, starting transfers between devices, gather_columns(): lax.all_to_all(jnp.stack(jnp.split(spread, lax.axis_size(axes), axis=1)),...  22.7 us
    all_to_all x2, waiting for transfers between devices, gather_columns(): lax.all_to_all(jnp.stack(jnp.split(spread, lax.axis_size(axes), axis=1)),...  12.3 us
    all_to_all x1, waiting for transfers between devices, on_device(): lax.all_to_all(outgoing, ('gy', 'gz'), split_axis=1, concat_axis=1, tiled...  11.3 us
    dot_general x1, matrix products, on_device(): jnp.einsum('plt,klt->kpt', picked, kind_hot, preferred_element_type=jnp.f...  9.96 us
    all_to_all x1, starting transfers between devices, on_device(): lax.all_to_all(outgoing, ('gy', 'gz'), split_axis=1, concat_axis=1, tiled...  7.68 us
    gather x1, local copies, waits for them, and re-layouts, on_device(): jnp.take(far_shift, coarse_kinds, axis=0).transpose(1, 0, 2)  6.81 us
  transfers between devices with their start and end apart: 3, of which 3 were waited for; matrix products, arithmetic and copies ran while one was open for 21% of the time, Pallas kernels for 0%

profile of v1, /device:TPU:8, one launch (start us, length us, event | category | flops | bytes accessed | tf_op | source)
XLA Modules:
  0.0 177.5 jit_solution(18127823725737857489)
XLA Ops:
  1.2 4.2 %reshape.170 = bf16[289,2312]{1,0:T(8,128)(2,1)} reshape(bf16[289,8,289]{2,1,0:T(8,128)(2,1)} %bitcast.291) | data formatting | bytes 2672672 | tf_op jit(solution)/shard_map/reshape | solution.py:13
  6.9 1.9 %convolution_reduce_fusion.1 = bf16[289]{0:T(512)(128)(2,1)S(1)} fusion(bf16[2312,1]{0,1:T(2,128)(2,1)S(1)} %reshape.216, bf16[289,2312]{1,0:T(8,128)(2,1)} %reshape.170), kind=kOutput, calls=%fused_computation.45 | convolution fusion | flops 1336336 | bytes 1341538 | tf_op jit(solution)/shard_map/dot_general | solution.py:14
  9.4 15.2 %all-to-all-start = ((bf16[16,289,1]{1,2,0:T(2,128)(2,1)}), bf16[16,289,1]{1,2,0:T(2,128)(2,1)S(1)}, u32[]{:S(2)}, u32[]{:S(2)}) async-start(bf16[16,289,1]{1,2,0:T(2,128)(2,1)} %stack.118), calls=%async_computation | async-start | bytes 49152 | tf_op jit(solution)/shard_map/all_to_all | solution.py:32
  25.0 3.9 %gather_fusion.2 = bf16[1024,289]{1,0:T(8,128)(2,1)S(1)} fusion(bf16[289,512]{0,1:T(8,128)(2,1)S(1)} %copy.70, s32[1024]{0:T(1024)S(1)} %get-tuple-element.8), kind=kCustom, calls=%fused_computation.2 | custom fusion | bytes 1187840 | tf_op jit(solution)/shard_map/jit(_take)/gather | solution.py:56
  30.2 7.0 %all-to-all-done = bf16[16,289,1]{1,2,0:T(2,128)(2,1)S(1)} async-done(((bf16[16,289,1]{1,2,0:T(2,128)(2,1)}), bf16[16,289,1]{1,2,0:T(2,128)(2,1)S(1)}, u32[]{:S(2)}, u32[]{:S(2)}) %all-to-all-start) | async-done | bytes 9280 | tf_op jit(solution)/shard_map/all_to_all | solution.py:32
  37.2 2.2 %fusion.60 = bf16[289,2]{0,1:T(2,128)(2,1)S(1)} fusion(bf16[289,8,289]{2,1,0:T(8,128)(2,1)} %bitcast.292, bf16[289,2,8]{0,2,1:T(8,128)(2,1)S(1)} %bitcast.302), kind=kOutput, calls=%fused_computation.46 | convolution fusion | flops 2673250 | bytes 1346740 | tf_op jit(solution)/shard_map/dot_general | solution.py:14
  58.1 7.5 %all-to-all-start.1 = ((bf16[32,289,2]{1,2,0:T(2,128)(2,1)}), bf16[32,289,2]{1,2,0:T(2,128)(2,1)S(1)}, u32[]{:S(2)}, u32[]{:S(2)}) async-start(bf16[32,289,2]{1,2,0:T(2,128)(2,1)} %constant_dynamic-update-slice_fusion), calls=%async_computation.1 | async-start | bytes 98304 | tf_op jit(solution)/shard_map/all_to_all | solution.py:32
  66.5 5.3 %all-to-all-done.1 = bf16[32,289,2]{1,2,0:T(2,128)(2,1)S(1)} async-done(((bf16[32,289,2]{1,2,0:T(2,128)(2,1)}), bf16[32,289,2]{1,2,0:T(2,128)(2,1)S(1)}, u32[]{:S(2)}, u32[]{:S(2)}) %all-to-all-start.1) | async-done | bytes 37024 | tf_op jit(solution)/shard_map/all_to_all | solution.py:32
  71.8 7.7 %all-to-all-start.2 = ((bf16[289,64,16]{0,2,1:T(8,128)(2,1)}), bf16[289,64,16]{0,2,1:T(8,128)(2,1)S(1)}, u32[]{:S(2)}, u32[]{:S(2)}) async-start(bf16[289,64,16]{0,2,1:T(8,128)(2,1)} %broadcast_select_fusion), calls=%async_computation.2 | async-start | bytes 1572864 | tf_op jit(solution)/shard_map/all_to_all | solution.py:57
  79.7 3.2 %copy.97 = bf16[289,8,289]{0,1,2:T(8,128)(2,1)} copy(bf16[289,8,289]{2,1,0:T(8,128)(2,1)S(1)} %bitcast.289) | data formatting | bytes 2672672 | tf_op jit(solution)/shard_map/transpose | solution.py:92
  82.9 6.8 %gather_fusion = bf16[8,289,289]{2,0,1:T(8,128)(2,1)} fusion(bf16[8,289,289]{2,0,1:T(8,128)(2,1)S(1)} %copy-done, s32[1024]{0:T(1024)S(1)} %get-tuple-element.7), kind=kCustom, calls=%fused_computation | custom fusion | bytes 2672704 | tf_op jit(solution)/shard_map/jit(_take)/gather | solution.py:69
  89.7 4.2 %copy.78 = bf16[8,289,289]{1,0,2:T(8,128)(2,1)} copy(bf16[8,289,289]{2,0,1:T(8,128)(2,1)} %param.11) | data formatting | bytes 2672672 | tf_op args[2]
  93.9 3.3 %reshape.175 = bf16[2312,289]{0,1:T(8,128)(2,1)S(1)} reshape(bf16[8,289,289]{1,0,2:T(8,128)(2,1)} %copy.78) | data formatting | bytes 2672672 | tf_op jit(solution)/shard_map/reshape | solution.py:21
  97.6 1.9 %constant_dynamic-slice_fusion = bf16[1,289,289]{2,0,1:T(2,128)(2,1)S(1)} fusion(bf16[8,289,289]{2,0,1:T(8,128)(2,1)} %param.11, s32[]{:T(128)S(6)} %select_n.79), kind=kLoop, calls=%fused_computation.141 | loop fusion | bytes 334088 | tf_op jit(solution)/shard_map/dynamic_slice | solution.py:77
  99.6 3.0 %select_bitcast_fusion = bf16[289,8,289]{2,1,0:T(8,128)(2,1)} fusion(bf16[8,289,289]{2,0,1:T(8,128)(2,1)} %gather_fusion, pred[8]{0:T(512)(128)(4,1)S(1)} %get-tuple-element.6), kind=kLoop, calls=%fused_computation.21 | loop fusion | flops 668168 | bytes 2672680 | tf_op jit(solution)/shard_map/jit(_take)/select_n | solution.py:69
  103.3 2.2 %fusion.57 = bf16[289]{0:T(512)(128)(2,1)S(1)} fusion(bf16[289,8,289]{2,1,0:T(8,128)(2,1)} %select_bitcast_fusion, bf16[8,289,1]{1,0,2:T(8,128)(2,1)S(1)} %select_bitcast_fusion.1), kind=kOutput, calls=%fused_computation.43 | convolution fusion | flops 1336336 | bytes 1341538 | tf_op jit(solution)/shard_map/dot_general | solution.py:74
  106.9 1.2 convolution_bitcast_fusion
  108.1 1.5 reshape.176
  110.7 11.3 %all-to-all-done.2 = bf16[289,64,16]{0,2,1:T(8,128)(2,1)S(1)} async-done(((bf16[289,64,16]{0,2,1:T(8,128)(2,1)}), bf16[289,64,16]{0,2,1:T(8,128)(2,1)S(1)}, u32[]{:S(2)}, u32[]{:S(2)}) %all-to-all-start.2) | async-done | bytes 591904 | tf_op jit(solution)/shard_map/all_to_all | solution.py:57
  122.2 33.2 %gather_fusion.3 = bf16[8192,289]{1,0:T(8,128)(2,1)} fusion(bf16[289,1536]{0,1:T(8,128)(2,1)S(1)} %pad_maximum_fusion, s32[8192]{0:T(1024)S(1)} %broadcast_clamp_fusion), kind=kCustom, calls=%fused_computation.3 | custom fusion | bytes 9502720 | tf_op jit(solution)/shard_map/jit(_take)/gather | solution.py:85
  155.4 10.0 %fusion = f32[512,8,289]{2,1,0:T(8,128)} fusion(bf16[16,512,289]{2,1,0:T(8,128)(2,1)} %bitcast.295, pred[16,512]{0,1:T(8,128)(4,1)S(1)} %copy.80, s32[16,512]{0,1:T(8,128)S(1)} %copy-done.6), kind=kOutput, calls=%fused_computation.4 | convolution fusion | flops 40312832 | bytes 9510912 | tf_op jit(solution)/shard_map/plt,klt->kpt/dot_general | solution.py:88
  165.4 6.5 %copy.86 = f32[512,8,289]{0,1,2:T(8,128)} copy(f32[512,8,289]{2,1,0:T(8,128)} %fusion) | data formatting | bytes 9469952 | tf_op jit(solution)/shard_map/plt,klt->kpt/dot_general | solution.py:88
  171.9 3.5 %convolution_bitcast_fusion.1 = f32[512,289]{0,1:T(8,128)S(1)} fusion(bf16[289,8,289]{0,1,2:T(8,128)(2,1)S(1)} %copy-done.4, f32[512,8,289]{0,1,2:T(8,128)} %copy.86), kind=kOutput, calls=%fused_computation.29 | convolution fusion | flops 684204032 | bytes 6663184 | tf_op jit(solution)/shard_map/dot_general | solution.py:93
  175.8 1.7 fusion.30
  (92 shorter events, 28.7 us)
Async XLA Ops:
  1.2 4.2 %copy-start.3 = (bf16[8,289,289]{2,0,1:T(8,128)(2,1)S(1)}, bf16[8,289,289]{2,0,1:T(8,128)(2,1)}, u32[]{:S(2)}) copy-start(bf16[8,289,289]{2,0,1:T(8,128)(2,1)} %param.10) | copy-start | bytes 4009012
  6.1 18.4 %copy-start.9 = (s32[1,1,64,16]{2,3,1,0:T(8,128)S(1)}, s32[1,1,64,16]{2,3,1,0:T(8,128)}, u32[]{:S(2)}) copy-start(s32[1,1,64,16]{2,3,1,0:T(8,128)} %param.13) | copy-start | bytes 12292
  6.2 18.6 %copy-start.10 = (s32[8,64]{1,0:T(8,128)S(1)}, s32[8,64]{1,0:T(8,128)}, u32[]{:S(2)}) copy-start(s32[8,64]{1,0:T(8,128)} %param.17) | copy-start | bytes 6148
  9.4 27.8 %all-to-all-start = ((bf16[16,289,1]{1,2,0:T(2,128)(2,1)}), bf16[16,289,1]{1,2,0:T(2,128)(2,1)S(1)}, u32[]{:S(2)}, u32[]{:S(2)}) async-start(bf16[16,289,1]{1,2,0:T(2,128)(2,1)} %stack.118), calls=%async_computation | async-start | bytes 49152 | tf_op jit(solution)/shard_map/all_to_all | solution.py:32
  29.0 36.6 %copy-start.7 = (s32[16,512]{1,0:T(8,128)S(1)}, s32[16,512]{1,0:T(8,128)}, u32[]{:S(2)}) copy-start(s32[16,512]{1,0:T(8,128)} %param.14) | copy-start | bytes 98308
  29.0 36.6 %copy-start.8 = (s32[16,512]{1,0:T(8,128)S(1)}, s32[16,512]{1,0:T(8,128)}, u32[]{:S(2)}) copy-start(s32[16,512]{1,0:T(8,128)} %param.15) | copy-start | bytes 98308
  37.2 42.5 %copy-start = (bf16[8,289,289]{2,0,1:T(8,128)(2,1)S(1)}, bf16[8,289,289]{2,0,1:T(8,128)(2,1)}, u32[]{:S(2)}) copy-start(bf16[8,289,289]{2,0,1:T(8,128)(2,1)} %param.12) | copy-start | bytes 4009012
  58.1 13.7 %all-to-all-start.1 = ((bf16[32,289,2]{1,2,0:T(2,128)(2,1)}), bf16[32,289,2]{1,2,0:T(2,128)(2,1)S(1)}, u32[]{:S(2)}, u32[]{:S(2)}) async-start(bf16[32,289,2]{1,2,0:T(2,128)(2,1)} %constant_dynamic-update-slice_fusion), calls=%async_computation.1 | async-start | bytes 98304 | tf_op jit(solution)/shard_map/all_to_all | solution.py:32
  71.8 50.3 %all-to-all-start.2 = ((bf16[289,64,16]{0,2,1:T(8,128)(2,1)}), bf16[289,64,16]{0,2,1:T(8,128)(2,1)S(1)}, u32[]{:S(2)}, u32[]{:S(2)}) async-start(bf16[289,64,16]{0,2,1:T(8,128)(2,1)} %broadcast_select_fusion), calls=%async_computation.2 | async-start | bytes 1572864 | tf_op jit(solution)/shard_map/all_to_all | solution.py:57
  93.9 3.3 %copy-start.11 = (s32[8,64]{1,0:T(8,128)S(1)}, s32[8,64]{1,0:T(8,128)}, u32[]{:S(2)}) copy-start(s32[8,64]{1,0:T(8,128)} %param.16) | copy-start | bytes 6148
  103.2 2.5 %copy-start.2 = (bf16[8,289,289]{2,0,1:T(8,128)(2,1)S(1)}, bf16[8,289,289]{2,0,1:T(8,128)(2,1)}, u32[]{:S(2)}) copy-start(bf16[8,289,289]{2,0,1:T(8,128)(2,1)} %param.11) | copy-start | bytes 4009012
  122.2 33.2 %copy-start.6 = (s32[16,512]{0,1:T(8,128)S(1)}, s32[16,512]{0,1:T(8,128)}, u32[]{:S(2)}) copy-start(s32[16,512]{0,1:T(8,128)} %copy.79) | copy-start | bytes 98308
  165.4 6.5 %copy-start.4 = (bf16[289,8,289]{0,1,2:T(8,128)(2,1)S(1)}, bf16[289,8,289]{0,1,2:T(8,128)(2,1)}, u32[]{:S(2)}) copy-start(bf16[289,8,289]{0,1,2:T(8,128)(2,1)} %copy.97) | copy-start | bytes 4009012
  171.9 3.8 %copy-start.1 = (f32[512,8,289]{0,1,2:T(8,128)S(1)}, f32[512,8,289]{0,1,2:T(8,128)}, u32[]{:S(2)}) copy-start(f32[512,8,289]{0,1,2:T(8,128)} %copy.86) | copy-start | bytes 14204932
  171.9 3.9 %copy-start.5 = (f32[289,512]{1,0:T(8,128)S(1)}, f32[289,512]{1,0:T(8,128)}, u32[]{:S(2)}) copy-start(f32[289,512]{1,0:T(8,128)} %copy.91) | copy-start | bytes 1775620
